TPU v7x, 256 devices: a whole 4x4x8 slice. The times are simulated.
256 devices in a mesh: dp: 16 (over y_lo, x, core), tensor: 16 (over y_hi, z).
Axes of the slice: x: 4, y: 4 (y_hi: 2, y_lo: 2; y = y_hi * 2 + y_lo), z: 8, core: 2. Of those that a mesh axis runs over, the one named last changes fastest.
Arguments:
- tokens: bfloat16 [12288, 8192], P(('dp', 'tensor')), may hold values from -6 to 6
- q_weight: bfloat16 [8192, 8192], P(None, 'tensor'), may hold values from -0.0625 to 0.0625
- pool_down: bfloat16 [128, 64, 8192], P('dp', None, 'tensor'), may hold values from -0.0625 to 0.0625
- pool_up: bfloat16 [128, 64, 8192], P('dp', None, 'tensor'), may hold values from -0.75 to 0.75
- block_units: int32 [16, 8], replicated, may hold values from 1 to 24, 48 in all within a row
- adapter_ids: int32 [16, 8], replicated, may hold values from 0 to 127, as said below
- location: int32 [128], replicated, may hold values from 0 to 127, as said below
Outputs:
- queries: bfloat16 [12288, 8192], P('dp', 'tensor')
Inputs may be any that keep to these rules, and one draw needn't show every extreme that they name: `adapter_ids`: the 8 adapters of one group lie in pool rows of 8 different dp shards (row location[a] lies on shard location[a] // 8). A permutation: adapter a is held in pool row location[a]. `block_units`: each group's blocks sum to 48; the largest is exactly 24.
All inputs are finite; a program needn't handle non-finite values.
Results may differ from a plain program's by a relative error of at most 0.0029.
Values may be sent and summed in bfloat16 or wider, within the bound.
No kernel may reach another device: no remote copies, remote signals or barrier semaphores. Data moves between devices by JAX's collectives and lax.ppermute only.
A program may use at most 128 MiB of HBM per device.

v0:
```python
import jax
import jax.numpy as jnp
from jax import lax
from jax.sharding import PartitionSpec as P

adapter_scale = 0.5


def tenant_mask(pool_unit_row, group_rows, tenants):
    block_ends = 16 * jnp.cumsum(pool_unit_row)
    positions = jnp.arange(group_rows, dtype=jnp.int32)
    tenant_index = jnp.sum((positions[:, None] >= block_ends[None, :]).astype(jnp.int32), axis=1)
    return tenant_index[:, None] == jnp.arange(tenants, dtype=jnp.int32)[None, :]


def on_device(tokens, q_weight, pool_down, pool_up, block_units, adapter_ids, location):
    my_group = lax.axis_index("dp")
    groups = adapter_ids.shape[0]
    tenants = adapter_ids.shape[1]
    pool_dev = pool_down.shape[0]
    rank_size = pool_down.shape[1]
    local_width = pool_down.shape[2]
    columns = q_weight.shape[1]
    slot_ids = jnp.take(location, adapter_ids, axis=0)
    slot_shard = slot_ids // pool_dev
    slot_row = slot_ids % pool_dev
    from_me = slot_shard == my_group
    send_row = jnp.sum(jnp.where(from_me, slot_row, 0), axis=1)
    both = jnp.concatenate([pool_down, pool_up], axis=1)
    send = jnp.take(both, send_row, axis=0)
    recv = lax.all_to_all(send, "dp", 0, 0, tiled=True)
    my_src = lax.dynamic_index_in_dim(slot_shard, my_group, 0, keepdims=False)
    panels = jnp.take(recv, my_src, axis=0)
    down_flat = panels[:, :rank_size, :].reshape(tenants * rank_size, local_width)
    up_flat = panels[:, rank_size:, :].reshape(tenants * rank_size, columns)
    width_start = lax.axis_index("tensor") * local_width
    row_block = lax.all_gather(tokens, "tensor", axis=0, tiled=True)
    base_projection = jnp.dot(row_block, q_weight, preferred_element_type=jnp.float32)
    local_cols = lax.dynamic_slice_in_dim(row_block, width_start, local_width, 1)
    wide_part = lax.dot_general(
        local_cols, down_flat, (((1,), (1,)), ((), ())), preferred_element_type=jnp.float32
    )
    group_rows = wide_part.shape[0]
    wide_part = wide_part.reshape(group_rows, tenants, rank_size)
    pool_unit_row = lax.dynamic_index_in_dim(block_units, my_group, 0, keepdims=False)
    tenant_masks = tenant_mask(pool_unit_row, group_rows, tenants)
    partial_low = jnp.sum(
        jnp.where(tenant_masks[:, :, None], wide_part, jnp.zeros((), jnp.float32)), axis=1
    )
    low_part = lax.psum_scatter(partial_low, "tensor", scatter_dimension=0, tiled=True)
    low_rank = lax.all_gather(low_part, "tensor", axis=0, tiled=True).astype(jnp.bfloat16)
    low_wide = jnp.where(
        tenant_masks[:, :, None], low_rank[:, None, :], jnp.zeros((), jnp.bfloat16)
    )
    adapter_contribution = jnp.dot(
        low_wide.reshape(group_rows, tenants * rank_size),
        up_flat,
        preferred_element_type=jnp.float32,
    )
    return (base_projection + adapter_scale * adapter_contribution).astype(jnp.bfloat16)


def solution(mesh):
    placed = (
        P(("dp", "tensor"), None),
        P(None, "tensor"),
        P("dp", None, "tensor"),
        P("dp", None, "tensor"),
        P(),
        P(),
        P(),
    )
    return jax.shard_map(
        on_device, mesh=mesh, in_specs=placed, out_specs=P("dp", "tensor"), check_vma=False
    )
```

profile of v0, /device:TPU:2, one launch (start us, length us, event | category | flops | bytes accessed | tf_op | source)
XLA Modules:
  0.0 472.1 jit_solution(14032850056442191799)
XLA Ops:
  6.5 0.7 all-gather.2.cloned.1.call-update
  7.3 0.8 copy.24
  8.0 0.1 reshape.115
  8.2 1.2 gather_fusion
  9.4 0.1 reshape.114
  9.5 0.1 add_select_fusion.1
  9.7 0.1 pad_maximum_fusion
  9.7 0.7 gather_fusion.1
  10.4 1.6 broadcast_select_fusion
  12.1 5.9 %all-to-all-start = ((bf16[16,128,512]{2,1,0:T(8,128)(2,1)}), bf16[16,128,512]{2,1,0:T(8,128)(2,1)S(1)}, u32[]{:S(2)}, u32[]{:S(2)}) async-start(bf16[16,128,512]{2,1,0:T(8,128)(2,1)} %broadcast_select_fusion), calls=%async_computation | async-start | bytes 4194304 | tf_op jit(solution)/shard_map/all_to_all | solution.py:31
  18.0 0.2 dynamic-slice_reduce_fusion
  18.2 0.2 reduce-window.8
  18.4 0.1 convert_reduce_fusion
  18.5 28.0 %all-to-all-done = bf16[16,128,512]{2,1,0:T(8,128)(2,1)S(1)} async-done(((bf16[16,128,512]{2,1,0:T(8,128)(2,1)}), bf16[16,128,512]{2,1,0:T(8,128)(2,1)S(1)}, u32[]{:S(2)}, u32[]{:S(2)}) %all-to-all-start) | async-done | bytes 2097184 | tf_op jit(solution)/shard_map/all_to_all | solution.py:31
  46.5 0.6 gather_fusion.2
  47.1 0.2 broadcast_select_fusion.1
  47.3 160.2 %all-gather.2.cloned.1.call-done = bf16[768,8192]{1,0:T(8,128)(2,1)} async-done(((bf16[48,8192]{1,0:T(8,128)(2,1)}), bf16[768,8192]{1,0:T(8,128)(2,1)}) %all-gather.2.cloned.1.call-update) | async-done | bytes 12582928 | tf_op jit(solution)/shard_map/all_gather | solution.py:37
  207.5 1.8 select_reduce_fusion
  209.3 0.9 copy.29
  210.2 201.0 %reduce-scatter.4.cloned.1.call-done = f32[48,64]{1,0:T(8,128)} async-done(((f32[768,64]{1,0:T(8,128)}), f32[48,64]{1,0:T(8,128)}) %reduce-scatter.4.cloned.1.call-update) | async-done | bytes 12304 | tf_op jit(solution)/shard_map/reduce_scatter | solution.py:50
  411.2 40.6 %all_gather.7 = f32[768,64]{1,0:T(8,128)S(1)} all-gather(f32[48,64]{1,0:T(8,128)} %reduce-scatter.4.cloned.1.call-done), channel_id=1, replica_groups=mesh['dp'=16,'tensor'=16] {'tensor'}, dimensions={0}, use_global_device_ids=true | all-gather | bytes 208896 | tf_op jit(solution)/shard_map/all_gather | solution.py:51
  451.8 0.1 copy.28
  451.9 0.6 fusion.3
  452.5 12.8 %fusion.1 = bf16[768,512]{1,0:T(8,128)(2,1)} fusion(f32[768,512,1]{1,0,2:T(8,128)S(1)} %fusion.3, bf16[768,8192]{1,0:T(8,128)(2,1)} %all-gather.2.cloned.1.call-done, bf16[8192,512]{1,0:T(8,128)(2,1)} %param.8), kind=kOutput, calls=%fused_computation.6 | convolution fusion | flops 6443630592 | bytes 23330816 | tf_op jit(solution)/shard_map/dot_general | solution.py:38
  (21 shorter events, 0.1 us)
Async XLA Ops:
  6.5 11.4 %copy-start = (s32[16,8]{0,1:T(8,128)S(1)}, s32[16,8]{0,1:T(8,128)}, u32[]{:S(2)}) copy-start(s32[16,8]{0,1:T(8,128)} %param.11) | copy-start | bytes 1540
  6.5 1.6 copy-start.1
  6.5 201.0 %all-gather.2.cloned.1.call-start = ((), (), s32[]{:S(2)}) async-start(), calls=%async_computation.2 | async-start | bytes 13369344 | tf_op jit(solution)/shard_map/all_gather | solution.py:37
  8.1 1.5 copy-start.2
  8.2 1.5 copy-start.3
  12.1 34.4 %all-to-all-start = ((bf16[16,128,512]{2,1,0:T(8,128)(2,1)}), bf16[16,128,512]{2,1,0:T(8,128)(2,1)S(1)}, u32[]{:S(2)}, u32[]{:S(2)}) async-start(bf16[16,128,512]{2,1,0:T(8,128)(2,1)} %broadcast_select_fusion), calls=%async_computation | async-start | bytes 4194304 | tf_op jit(solution)/shard_map/all_to_all | solution.py:31
  17.9 393.3 %reduce-scatter.4.cloned.1.call-start = ((), (), s32[]{:S(2)}) async-start(), calls=%async_computation.3 | async-start | bytes 417792 | tf_op jit(solution)/shard_map/reduce_scatter | solution.py:50
Sparse Core Ops, SparseCore 0:
  9.9 197.5 all-gather.1
  211.3 199.8 reduce-scatter.3
where the time goes:
time: 472 us
  waiting for transfers between devices  390 us (83%)
  blocking collectives  40.6 us (9%)
  matrix products  15.1 us (3%)
  between operations  13.6 us (3%)
  starting transfers between devices  5.9 us (1%)
    reduce_scatter x1, waiting for transfers between devices, on_device(): lax.psum_scatter(partial_low, 'tensor', scatter_dimension=0, tiled=True)  201 us
    all_gather x1, waiting for transfers between devices, on_device(): row_block = lax.all_gather(tokens, 'tensor', axis=0, tiled=True)  160 us
    all_gather x1, blocking collectives, on_device(): lax.all_gather(low_part, 'tensor', axis=0, tiled=True).astype(jnp.bfloat16)  40.6 us
    all_to_all x1, waiting for transfers between devices, on_device(): recv = lax.all_to_all(send, 'dp', 0, 0, tiled=True)  28 us
    dot_general x1, matrix products, on_device(): jnp.dot(row_block, q_weight, preferred_element_type=jnp.float32)  12.8 us
  transfers between devices with their start and end apart: 3, of which 3 were waited for; matrix products, arithmetic and copies ran while one was open for 1% of the time, Pallas kernels for 0%

commit v1 on v0

--- a/solution.py
+++ b/solution.py
@@ -34,7 +34,9 @@
     down_flat = panels[:, :rank_size, :].reshape(tenants * rank_size, local_width)
     up_flat = panels[:, rank_size:, :].reshape(tenants * rank_size, columns)
     width_start = lax.axis_index("tensor") * local_width
-    row_block = lax.all_gather(tokens, "tensor", axis=0, tiled=True)
+    row_block = jnp.concatenate(
+        lax.all_to_all(jnp.stack([tokens] * lax.psum(1, "tensor")), "tensor", 0, 0), axis=0
+    )
     base_projection = jnp.dot(row_block, q_weight, preferred_element_type=jnp.float32)
     local_cols = lax.dynamic_slice_in_dim(row_block, width_start, local_width, 1)
     wide_part = lax.dot_general(

time: 472 us -> 614 us (1.30)
  waiting for transfers between devices: 390 us -> 491 us
  blocking collectives: 40.6 us -> 70.7 us
    all_to_all x1, waiting for transfers between devices: 28 us -> 279 us  [on_device(): lax.all_to_all(jnp.stack([tokens] * lax.psum(1, 'tensor')), 'tensor', 0, 0)]
    all_gather x1 -> x0, waiting for transfers between devices: 160 us -> none  [on_device(): row_block = lax.all_gather(tokens, 'tensor', axis=0, tiled=True)]
    all_to_all x0 -> x1, blocking collectives: none -> 30.2 us  [on_device(): recv = lax.all_to_all(send, 'dp', 0, 0, tiled=True)]
    reduce_scatter x1, waiting for transfers between devices: 201 us -> 213 us  [on_device(): lax.psum_scatter(partial_low, 'tensor', scatter_dimension=0, tiled=True)]
  transfers between devices with their start and end apart: 3 -> 2, of which waited for: 3 -> 2; matrix products, arithmetic and copies ran while one was open for 1% -> 0% of each run, Pallas kernels for 0% -> 0%
where the time goes in v1:
time: 614 us; the launch traced here: 613 us
  waiting for transfers between devices  491 us (80%)
  blocking collectives  70.7 us (12%)
  matrix products  15.1 us (2%)
  between operations  13.6 us (2%)
  starting transfers between devices  11 us (2%)
  local copies, waits for them, and re-layouts  10.7 us (2%)
    all_to_all x1, waiting for transfers between devices, on_device(): lax.all_to_all(jnp.stack([tokens] * lax.psum(1, 'tensor')), 'tensor', 0, 0)  279 us
    reduce_scatter x1, waiting for transfers between devices, on_device(): lax.psum_scatter(partial_low, 'tensor', scatter_dimension=0, tiled=True)  213 us
    all_gather x1, blocking collectives, on_device(): lax.all_gather(low_part, 'tensor', axis=0, tiled=True).astype(jnp.bfloat16)  40.5 us
    all_to_all x1, blocking collectives, on_device(): recv = lax.all_to_all(send, 'dp', 0, 0, tiled=True)  30.2 us
    dot_general x1, matrix products, on_device(): jnp.dot(row_block, q_weight, preferred_element_type=jnp.float32)  12.8 us
  transfers between devices with their start and end apart: 2, of which 2 were waited for; matrix products, arithmetic and copies ran while one was open for 0% of the time, Pallas kernels for 0%

profile of v1, /device:TPU:2, one launch (start us, length us, event | category | flops | bytes accessed | tf_op | source)
XLA Modules:
  0.0 613.4 jit_solution(8229870156523953904)
XLA Ops:
  6.5 0.8 copy.24
  7.3 0.1 reshape.121
  7.5 1.2 gather_fusion
  8.7 0.1 reshape.120
  8.8 0.1 add_select_fusion.1
  9.0 0.1 pad_maximum_fusion
  9.1 0.7 gather_fusion.1
  9.7 0.3 broadcast_select_fusion
  10.0 30.2 %all_to_all.10 = bf16[16,128,512]{2,1,0:T(8,128)(2,1)S(1)} all-to-all(bf16[16,128,512]{2,1,0:T(8,128)(2,1)S(1)} %broadcast_select_fusion), channel_id=1, replica_groups=mesh['dp'=16,'tensor'=16] {'dp'}, dimensions={0} | all-to-all | bytes 4194304 | tf_op jit(solution)/shard_map/all_to_all | solution.py:31
  40.2 6.0 stack.2
  46.3 11.0 %all-to-all-start = ((bf16[16,48,8192]{2,1,0:T(8,128)(2,1)}), bf16[16,48,8192]{2,1,0:T(8,128)(2,1)}, u32[]{:S(2)}, u32[]{:S(2)}) async-start(bf16[16,48,8192]{2,1,0:T(8,128)(2,1)} %stack.2), calls=%async_computation | async-start | bytes 25165824 | tf_op jit(solution)/shard_map/all_to_all | solution.py:38
  57.3 0.2 dynamic-slice_reduce_fusion
  57.5 0.2 reduce-window.8
  57.7 0.1 convert_reduce_fusion
  57.8 0.6 gather_fusion.2
  58.4 0.2 broadcast_select_fusion.1
  58.6 278.6 %all-to-all-done = bf16[16,48,8192]{2,1,0:T(8,128)(2,1)} async-done(((bf16[16,48,8192]{2,1,0:T(8,128)(2,1)}), bf16[16,48,8192]{2,1,0:T(8,128)(2,1)}, u32[]{:S(2)}, u32[]{:S(2)}) %all-to-all-start) | async-done | bytes 12582944 | tf_op jit(solution)/shard_map/all_to_all | solution.py:38
  337.2 1.8 select_reduce_fusion
  339.0 0.9 copy.29
  339.9 212.6 %reduce-scatter.4.cloned.1.call-done = f32[48,64]{1,0:T(8,128)} async-done(((f32[768,64]{1,0:T(8,128)}), f32[48,64]{1,0:T(8,128)}) %reduce-scatter.4.cloned.1.call-update) | async-done | bytes 12304 | tf_op jit(solution)/shard_map/reduce_scatter | solution.py:52
  552.5 40.5 %all_gather.3 = f32[768,64]{1,0:T(8,128)S(1)} all-gather(f32[48,64]{1,0:T(8,128)} %reduce-scatter.4.cloned.1.call-done), channel_id=1, replica_groups=mesh['dp'=16,'tensor'=16] {'tensor'}, dimensions={0}, use_global_device_ids=true | all-gather | bytes 208896 | tf_op jit(solution)/shard_map/all_gather | solution.py:53
  593.0 0.1 copy.28
  593.1 0.6 fusion.3
  593.8 12.8 %fusion.1 = bf16[768,512]{1,0:T(8,128)(2,1)} fusion(f32[768,512,1]{1,0,2:T(8,128)S(1)} %fusion.3, bf16[768,8192]{1,0:T(8,128)(2,1)} %bitcast, bf16[8192,512]{1,0:T(8,128)(2,1)} %param.8), kind=kOutput, calls=%fused_computation.6 | convolution fusion | flops 6443630592 | bytes 23330816 | tf_op jit(solution)/shard_map/dot_general | solution.py:40
  (22 shorter events, 0.2 us)
Async XLA Ops:
  6.5 50.7 %copy-start = (s32[16,8]{0,1:T(8,128)S(1)}, s32[16,8]{0,1:T(8,128)}, u32[]{:S(2)}) copy-start(s32[16,8]{0,1:T(8,128)} %param.11) | copy-start | bytes 1540
  6.5 0.9 copy-start.1
  7.4 1.5 copy-start.3
  7.5 1.5 copy-start.4
  10.0 30.2 %copy-start.2 = (bf16[48,8192]{1,0:T(8,128)(2,1)S(1)}, bf16[48,8192]{1,0:T(8,128)(2,1)}, u32[]{:S(2)}) copy-start(bf16[48,8192]{1,0:T(8,128)(2,1)} %param.7) | copy-start | bytes 2359300
  46.3 291.0 %all-to-all-start = ((bf16[16,48,8192]{2,1,0:T(8,128)(2,1)}), bf16[16,48,8192]{2,1,0:T(8,128)(2,1)}, u32[]{:S(2)}, u32[]{:S(2)}) async-start(bf16[16,48,8192]{2,1,0:T(8,128)(2,1)} %stack.2), calls=%async_computation | async-start | bytes 25165824 | tf_op jit(solution)/shard_map/all_to_all | solution.py:38
  57.2 495.3 %reduce-scatter.4.cloned.1.call-start = ((), (), s32[]{:S(2)}) async-start(), calls=%async_computation.3 | async-start | bytes 417792 | tf_op jit(solution)/shard_map/reduce_scatter | solution.py:52
Sparse Core Ops, SparseCore 0:
  340.1 212.4 reduce-scatter.3
